TPU v7x, 128 devices: a whole 4x4x4 slice. The times are simulated.
128 devices in a mesh: row: 8 (over x, core), col: 4 (over z), depth: 4 (over y).
Axes of the slice: x: 4, y: 4, z: 4, core: 2. Of those that a mesh axis runs over, the one named last changes fastest.
Arguments:
- tokens: bfloat16 [1024, 8192], P(('col', 'depth'), 'row'), may hold values from -6 to 6
- gate_weight: bfloat16 [8192, 14336], P('row', ('col', 'depth')), may hold values from -0.109375 to 0.109375
- up_weight: bfloat16 [8192, 14336], P('row', ('col', 'depth')), may hold values from -0.109375 to 0.109375
- down_weight: bfloat16 [14336, 8192], P(('col', 'depth'), 'row'), may hold values from -0.078125 to 0.078125
- gate_mask: int32 [64, 112], P('row', ('col', 'depth')), may hold values 0 or 1
- up_mask: int32 [64, 112], P('row', ('col', 'depth')), may hold values 0 or 1
- down_mask: int32 [112, 64], P(('col', 'depth'), 'row'), may hold values 0 or 1
- grad_out: bfloat16 [1024, 8192], P(('col', 'depth'), 'row'), may hold values from -1.5 to 1.5
Outputs:
- mixed: bfloat16 [1024, 8192], P(('col', 'depth'), 'row')
- grad_tokens: bfloat16 [1024, 8192], P(('col', 'depth'), 'row')
- grad_gate_weight: bfloat16 [8192, 14336], P('row', ('col', 'depth'))
- grad_up_weight: bfloat16 [8192, 14336], P('row', ('col', 'depth'))
- grad_down_weight: bfloat16 [14336, 8192], P(('col', 'depth'), 'row')
Inputs may be any that keep to these rules, and one draw needn't show every extreme that they name: `gate_mask`: 1 keeps the 128 x 128 block of the gate projection, 0 zeroes it. `up_mask`: 1 keeps the 128 x 128 block of the up projection, 0 zeroes it. `down_mask`: 1 keeps the 128 x 128 block of the down projection, 0 zeroes it.
All inputs are finite; a program needn't handle non-finite values.
Results may differ from a plain program's by a relative error of at most 0.015.
Values may be sent and summed in bfloat16 or wider, within the bound.
No kernel may reach another device: no remote copies, remote signals or barrier semaphores. Data moves between devices by JAX's collectives and lax.ppermute only.
A program may use at most 128 MiB of HBM per device.

v0:
```python
import jax
import jax.numpy as jnp
from jax import lax
from jax.sharding import PartitionSpec as P

BLK = 128


def expand(mask):
    return jnp.repeat(jnp.repeat(mask, BLK, axis=0), BLK, axis=1) > 0


def swiglu(sums):
    width = sums.shape[1] // 2
    gate = sums[:, :width]
    up = sums[:, width:]
    sig = jax.nn.sigmoid(gate)
    return (gate * sig * up).astype(jnp.bfloat16)


def swiglu_back(sums, grad_act):
    width = sums.shape[1] // 2
    gate = sums[:, :width]
    up = sums[:, width:]
    sig = jax.nn.sigmoid(gate)
    grad_gate = grad_act * up * sig * (1.0 + gate * (1.0 - sig))
    grad_up = grad_act * gate * sig
    return jnp.concatenate([grad_gate, grad_up], axis=1).astype(jnp.bfloat16)


def row_sums(term, rows):
    return lax.psum_scatter(
        term(jnp.int32(0), lax.axis_size("row") * rows), "row", scatter_dimension=0, tiled=True
    )


def row_gather(block):
    return lax.all_gather(block, "row", axis=0, tiled=True)


def row_sums_direct(full):
    parts = lax.axis_size("row")
    rows = full.shape[0] // parts
    pieces = lax.all_to_all(
        full.astype(jnp.bfloat16).reshape((parts, rows) + full.shape[1:]), "row", 0, 0
    )
    return jnp.sum(pieces.astype(jnp.float32), axis=0)


def row_sums_paired(full):
    parts = lax.axis_size("row")
    chips = parts // 2
    rows = full.shape[0] // parts
    member = lax.axis_index("row")
    core = member % 2
    chip = member // 2
    blocks = full.reshape((chips, 2, rows) + full.shape[1:])
    give = jnp.take(blocks, 1 - core, axis=1)
    keep = jnp.take(blocks, core, axis=1)
    moved_in = lax.ppermute(give.astype(jnp.bfloat16), "row", [(i, i ^ 1) for i in range(parts)])
    pair = keep + moved_in.astype(jnp.float32)
    sent = pair.astype(jnp.bfloat16)
    total = jnp.take(pair, chip, axis=0)
    for hop in range(1, chips):
        piece = jnp.take(sent, (chip + hop) % chips, axis=0)
        moved = lax.ppermute(piece, "row", [(i, (i + 2 * hop) % parts) for i in range(parts)])
        total = total + moved.astype(jnp.float32)
    return total


def row_gather_direct(block):
    parts = lax.axis_size("row")
    copies = jnp.broadcast_to(block[None], (parts,) + block.shape)
    pieces = lax.all_to_all(copies, "row", 0, 0)
    return pieces.reshape((parts * block.shape[0],) + block.shape[1:])


def group_sums(term, rows):
    parts = lax.axis_size(("col", "depth"))
    full = term(jnp.int32(0), rows * parts).astype(jnp.bfloat16)
    pieces = lax.all_to_all(full.reshape((parts, rows) + full.shape[1:]), ("col", "depth"), 0, 0)
    return jnp.sum(pieces.astype(jnp.float32), axis=0)


def group_gather(block):
    parts = lax.axis_size(("col", "depth"))
    copies = jnp.broadcast_to(block[None], (parts,) + block.shape)
    pieces = lax.all_to_all(copies, ("col", "depth"), 0, 0)
    return pieces.reshape((parts * block.shape[0],) + block.shape[1:])


def local(tokens, gate_weight, up_weight, down_weight, gate_mask, up_mask, down_mask, grad_out):
    zero_value = jnp.zeros((), jnp.bfloat16)
    keep_gate = expand(gate_mask)
    keep_up = expand(up_mask)
    keep_down = expand(down_mask)
    w_both = jnp.concatenate(
        [jnp.where(keep_gate, gate_weight, zero_value), jnp.where(keep_up, up_weight, zero_value)],
        axis=1,
    )
    w_down = jnp.where(keep_down, down_weight, zero_value)
    x_all = group_gather(tokens)
    split_rows = x_all.shape[0] // lax.axis_size("row")
    own_rows = tokens.shape[0]
    inner = (((0,), (0,)), ((), ()))
    outer = (((1,), (1,)), ((), ()))
    hidden = jnp.dot(x_all, w_both, preferred_element_type=jnp.float32)
    sums = row_sums(lambda start, count: hidden, split_rows)
    grad_out, _ = lax.optimization_barrier((grad_out, hidden))
    grad_all = group_gather(grad_out)
    act_partial = lax.dot_general(grad_all, w_down, outer, preferred_element_type=jnp.float32)
    act_sums, act_partial = lax.optimization_barrier((sums, act_partial))
    act_all = row_gather(swiglu(act_sums))

    def out_term(start, count):
        return jnp.dot(act_all, w_down, preferred_element_type=jnp.float32)

    mixed = group_sums(out_term, own_rows).astype(jnp.bfloat16)
    grad_down = lax.dot_general(act_all, grad_all, inner, preferred_element_type=jnp.float32)
    grad_down_weight = jnp.where(keep_down, grad_down, jnp.float32(0.0)).astype(jnp.bfloat16)
    grad_act = row_sums_paired(act_partial)
    held_sums, grad_act, _ = lax.optimization_barrier((sums, grad_act, act_all))
    grads_all = row_gather(swiglu_back(held_sums, grad_act))
    grad_both = lax.dot_general(x_all, grads_all, inner, preferred_element_type=jnp.float32)
    width = grad_both.shape[1] // 2
    grad_gate_weight = jnp.where(keep_gate, grad_both[:, :width], jnp.float32(0.0)).astype(
        jnp.bfloat16
    )
    grad_up_weight = jnp.where(keep_up, grad_both[:, width:], jnp.float32(0.0)).astype(jnp.bfloat16)

    def input_term(start, count):
        return lax.dot_general(grads_all, w_both, outer, preferred_element_type=jnp.float32)

    grad_tokens = group_sums(input_term, own_rows).astype(jnp.bfloat16)
    return (mixed, grad_tokens, grad_gate_weight, grad_up_weight, grad_down_weight)


def solution(mesh):
    return jax.shard_map(
        local,
        mesh=mesh,
        in_specs=(
            P(("col", "depth"), "row"),
            P("row", ("col", "depth")),
            P("row", ("col", "depth")),
            P(("col", "depth"), "row"),
            P("row", ("col", "depth")),
            P("row", ("col", "depth")),
            P(("col", "depth"), "row"),
            P(("col", "depth"), "row"),
        ),
        out_specs=(
            P(("col", "depth"), "row"),
            P(("col", "depth"), "row"),
            P("row", ("col", "depth")),
            P("row", ("col", "depth")),
            P(("col", "depth"), "row"),
        ),
        check_vma=False,
    )
```

profile of v0, /device:TPU:1, one launch (start us, length us, event | category | flops | bytes accessed | tf_op | source)
XLA Modules:
  0.0 234.1 jit_solution(18047022158019151847)
XLA Ops:
  7.2 2.5 %broadcast_in_dim.83 = bf16[16,64,1024]{2,1,0:T(8,128)(2,1)} broadcast(bf16[64,1024]{1,0:T(8,128)(2,1)} %param.12), dimensions={1,2} | broadcast | bytes 2228224 | tf_op jit(solution)/shard_map/broadcast_in_dim | solution.py:87
  9.7 8.8 %all-to-all-start = ((bf16[16,64,1024]{2,1,0:T(8,128)(2,1)}), bf16[16,64,1024]{2,1,0:T(8,128)(2,1)}, u32[]{:S(2)}, u32[]{:S(2)}) async-start(bf16[16,64,1024]{2,1,0:T(8,128)(2,1)} %broadcast_in_dim.83), calls=%async_computation | async-start | bytes 4194304 | tf_op jit(solution)/shard_map/all_to_all | solution.py:88
  18.5 0.1 copy.19
  18.6 0.1 copy.21
  18.7 0.1 broadcast_bitcast_fusion
  18.9 2.9 %copy.20 = bf16[1024,896]{0,1:T(8,128)(2,1)S(1)} copy(bf16[1024,896]{1,0:T(8,128)(2,1)} %param.13) | data formatting | bytes 3670016 | tf_op args[1]
  21.8 3.8 %copy.22 = bf16[1024,896]{0,1:T(8,128)(2,1)} copy(bf16[1024,896]{1,0:T(8,128)(2,1)} %param.14) | data formatting | bytes 3670016 | tf_op args[2]
  25.6 3.6 %bitcast_select_fusion.1 = (bf16[1024,896]{0,1:T(8,128)(2,1)}, bf16[1024,896]{0,1:T(8,128)(2,1)}) fusion(bf16[1024,896]{0,1:T(8,128)(2,1)} %copy.22, pred[1024,7]{0,1:T(8,128)(4,1)S(1)} %bitcast.75, bf16[1024,896]{0,1:T(8,128)(2,1)S(1)} %copy.20, pred[1024,7]{0,1:T(8,128)(4,1)S(1)} %bitcast.77), kind=kLoop, calls=%fused_computation.1 | loop fusion | flops 1835008 | bytes 7354368 | tf_op jit(solution)/shard_map/jit(_where)/select_n | solution.py:98
  29.2 20.2 %all-to-all-done = bf16[16,64,1024]{2,1,0:T(8,128)(2,1)} async-done(((bf16[16,64,1024]{2,1,0:T(8,128)(2,1)}), bf16[16,64,1024]{2,1,0:T(8,128)(2,1)}, u32[]{:S(2)}, u32[]{:S(2)}) %all-to-all-start) | async-done | bytes 2097184 | tf_op jit(solution)/shard_map/all_to_all | solution.py:88
  49.5 9.7 %convolution_bitcast_fusion.1 = f32[1024,1792]{0,1:T(8,128)} fusion(bf16[1024,1024]{1,0:T(8,128)(2,1)} %bitcast.2, bf16[1024,896]{0,1:T(8,128)(2,1)} %get-tuple-element.69, bf16[1024,896]{0,1:T(8,128)(2,1)} %get-tuple-element.70), kind=kOutput, calls=%fused_computation.5 | convolution fusion | flops 3765436416 | bytes 13107200 | tf_op jit(solution)/shard_map/dot_general | solution.py:107
  59.1 0.9 copy-done.3
  60.0 1.7 broadcast_in_dim.84
  61.7 3.9 %all-to-all-start.1 = ((bf16[16,64,1024]{2,1,0:T(8,128)(2,1)}), bf16[16,64,1024]{2,1,0:T(8,128)(2,1)S(1)}, u32[]{:S(2)}, u32[]{:S(2)}) async-start(bf16[16,64,1024]{2,1,0:T(8,128)(2,1)} %broadcast_in_dim.84), calls=%async_computation.2 | async-start | bytes 4194304 | tf_op jit(solution)/shard_map/all_to_all | solution.py:88
  65.7 28.5 %all-to-all-done.1 = bf16[16,64,1024]{2,1,0:T(8,128)(2,1)S(1)} async-done(((bf16[16,64,1024]{2,1,0:T(8,128)(2,1)}), bf16[16,64,1024]{2,1,0:T(8,128)(2,1)S(1)}, u32[]{:S(2)}, u32[]{:S(2)}) %all-to-all-start.1) | async-done | bytes 2097184 | tf_op jit(solution)/shard_map/all_to_all | solution.py:88
  94.3 2.8 %broadcast_in_dim.86 = pred[896,8,128]{2,1,0:T(8,128)(4,1)S(1)} broadcast(pred[896,8]{1,0:T(8,128)(4,1)S(1)} %bitcast.74), dimensions={0,1} | broadcast | bytes 924672 | tf_op jit(solution)/shard_map/broadcast_in_dim | solution.py:10
  97.1 5.9 %fusion.4 = f32[1024,896]{1,0:T(8,128)} fusion(bf16[1024,1024]{1,0:T(8,128)(2,1)S(1)} %bitcast.65, bf16[896,1024]{1,0:T(8,128)(2,1)} %param.15, pred[112,8,8,128]{3,2,1,0:T(8,128)(4,1)S(1)} %bitcast.71), kind=kOutput, calls=%fused_computation.16 | convolution fusion | flops 1879965696 | bytes 8519680 | tf_op jit(solution)/shard_map/dot_general | solution.py:111
  103.0 2.1 reduce-scatter.2.cloned.1.call-done
  105.1 2.0 multiply_convert_fusion.2
  107.2 1.6 constant_dynamic-slice_fusion
  108.8 0.6 copy.28
  109.4 1.1 bitcast_convert_fusion
  110.6 1.2 collective-permute-start
  111.8 2.8 %constant_dynamic-slice_fusion.1 = f32[4,1,128,896]{3,2,1,0:T(8,128)} fusion(f32[4,2,128,896]{3,2,1,0:T(8,128)} %bitcast.70, s32[]{:T(128)S(6)} %select_n.92), kind=kLoop, calls=%fused_computation.38 | loop fusion | bytes 3670020 | tf_op jit(solution)/shard_map/jit(_take) | solution.py:59
  114.6 1.8 copy.27
  116.4 2.7 %fusion.13 = (bf16[4,128,896]{1,2,0:T(8,128)(2,1)S(1)}, f32[4,128,896]{1,2,0:T(8,128)}) fusion(bf16[4,128,896]{1,2,0:T(8,128)(2,1)} %collective-permute-done, f32[4,1,128,896]{2,3,0,1:T(8,128)S(1)} %copy.27, pred[]{:T(512)S(6)} %and.48), kind=kLoop, calls=%fused_computation.43 | loop fusion | flops 1835008 | bytes 5505025 | tf_op jit(solution)/shard_map/convert_element_type | solution.py:62
  119.2 1.1 collective-permute-start.1
  120.3 1.7 collective-permute-start.3
  121.9 1.3 collective-permute-start.2
  123.3 7.4 %collective-permute-done.1 = bf16[128,896]{0,1:T(8,128)(2,1)S(1)} collective-permute-done((bf16[128,896]{0,1:T(8,128)(2,1)S(1)}, bf16[128,896]{0,1:T(8,128)(2,1)S(1)}, u32[]{:S(2)}, u32[]{:S(2)}) %collective-permute-start.1) | collective-permute-done | bytes 229408 | tf_op jit(solution)/shard_map/ppermute | solution.py:66
  130.7 7.5 %collective-permute-done.2 = bf16[128,896]{0,1:T(8,128)(2,1)S(1)} collective-permute-done((bf16[128,896]{0,1:T(8,128)(2,1)S(1)}, bf16[128,896]{0,1:T(8,128)(2,1)S(1)}, u32[]{:S(2)}, u32[]{:S(2)}) %collective-permute-start.2) | collective-permute-done | bytes 229408 | tf_op jit(solution)/shard_map/ppermute | solution.py:66
  138.3 1.1 fusion.8
  139.4 0.2 multiply_convert_fusion.1
  139.7 0.8 pad_maximum_fusion.5
  140.5 5.8 %convolution_convert_fusion = bf16[1024,1024]{1,0:T(8,128)(2,1)} fusion(bf16[1024,896]{0,1:T(8,128)(2,1)} %all-gather.3.cloned.1.call-done, bf16[896,1024]{1,0:T(8,128)(2,1)} %param.15, pred[112,8,8,128]{3,2,1,0:T(8,128)(4,1)S(1)} %bitcast.72), kind=kOutput, calls=%fused_computation.13 | convolution fusion | flops 1881014272 | bytes 6684672 | tf_op jit(solution)/shard_map/dot_general | solution.py:116
  146.3 7.7 %all-to-all-start.2 = ((bf16[16,64,1024]{2,1,0:T(8,128)(2,1)}), bf16[16,64,1024]{2,1,0:T(8,128)(2,1)S(1)}, u32[]{:S(2)}, u32[]{:S(2)}) async-start(bf16[16,64,1024]{2,1,0:T(8,128)(2,1)} %bitcast.68), calls=%async_computation.3 | async-start | bytes 4194304 | tf_op jit(solution)/shard_map/all_to_all | solution.py:81
  154.1 23.3 %all-gather.5.cloned.1.call-done = bf16[1024,1792]{0,1:T(8,128)(2,1)} async-done(((bf16[128,1792]{0,1:T(8,128)(2,1)}), bf16[1024,1792]{0,1:T(8,128)(2,1)}) %all-gather.5.cloned.1.call-update) | async-done | bytes 3670032 | tf_op jit(solution)/shard_map/all_gather | solution.py:38
  177.4 8.5 %fusion.3 = bf16[1024,1024]{1,0:T(8,128)(2,1)} fusion(bf16[1024,1792]{0,1:T(8,128)(2,1)} %all-gather.5.cloned.1.call-done, bf16[1024,896]{0,1:T(8,128)(2,1)} %get-tuple-element.69, bf16[1024,896]{0,1:T(8,128)(2,1)} %get-tuple-element.70), kind=kOutput, calls=%fused_computation.12 | convolution fusion | flops 3766484992 | bytes 9437184 | tf_op jit(solution)/shard_map/dot_general | solution.py:132
  185.9 0.8 all-to-all-done.2
  186.7 1.3 copy-done
  188.0 5.9 %all-to-all-start.3 = ((bf16[16,64,1024]{2,1,0:T(8,128)(2,1)}), bf16[16,64,1024]{2,1,0:T(8,128)(2,1)S(1)}, u32[]{:S(2)}, u32[]{:S(2)}) async-start(bf16[16,64,1024]{2,1,0:T(8,128)(2,1)} %bitcast.67), calls=%async_computation.4 | async-start | bytes 4194304 | tf_op jit(solution)/shard_map/all_to_all | solution.py:81
  193.9 5.5 %select_convert_fusion = bf16[896,1024]{1,0:T(8,128)(2,1)} fusion(pred[112,8,8,128]{3,2,1,0:T(8,128)(4,1)S(1)} %bitcast.73, bf16[1024,896]{0,1:T(8,128)(2,1)} %all-gather.3.cloned.1.call-done, bf16[1024,1024]{1,0:T(8,128)(2,1)} %bitcast.66), kind=kOutput, calls=%fused_computation.9 | convolution fusion | flops 1880883200 | bytes 6684672 | tf_op jit(solution)/shard_map/dot_general | solution.py:119
  199.4 2.7 %reduce_sum.24 = bf16[64,1024]{1,0:T(8,128)(2,1)} reduce(bf16[16,64,1024]{2,1,0:T(8,128)(2,1)} %copy-done, bf16[]{:T(256)} %constant.84.clone.1), dimensions={0}, to_apply=%region_1.2 | reduce | flops 983040 | bytes 2228226 | tf_op jit(solution)/shard_map/reduce_sum | solution.py:82
  202.1 6.7 %convolution_bitcast_fusion = bf16[1024,1792]{0,1:T(8,128)(2,1)S(1)} fusion(bf16[1024,1792]{0,1:T(8,128)(2,1)} %all-gather.5.cloned.1.call-done, bf16[1024,1024]{1,0:T(8,128)(2,1)} %bitcast.2), kind=kOutput, calls=%fused_computation.4 | convolution fusion | flops 3758096384 | bytes 9437184 | tf_op jit(solution)/shard_map/dot_general | solution.py:124
  208.7 3.0 %fusion.1 = (bf16[1024,896]{0,1:T(8,128)(2,1)}, bf16[1024,896]{0,1:T(8,128)(2,1)}) fusion(bf16[1024,1792]{0,1:T(8,128)(2,1)S(1)} %convolution_bitcast_fusion, pred[1024,7]{0,1:T(8,128)(4,1)S(1)} %bitcast.76, pred[1024,7]{0,1:T(8,128)(4,1)S(1)} %bitcast.78), kind=kLoop, calls=%fused_computation.7 | loop fusion | flops 1835008 | bytes 7354368 | tf_op jit(solution)/shard_map/convert_element_type | solution.py:129
  211.7 3.8 %copy.26 = bf16[1024,896]{1,0:T(8,128)(2,1)} copy(bf16[1024,896]{0,1:T(8,128)(2,1)} %get-tuple-element.62) | data formatting | bytes 3670016
  215.5 3.8 %copy.25 = bf16[1024,896]{1,0:T(8,128)(2,1)} copy(bf16[1024,896]{0,1:T(8,128)(2,1)} %get-tuple-element.63) | data formatting | bytes 3670016
  219.3 7.2 %all-to-all-done.3 = bf16[16,64,1024]{2,1,0:T(8,128)(2,1)S(1)} async-done(((bf16[16,64,1024]{2,1,0:T(8,128)(2,1)}), bf16[16,64,1024]{2,1,0:T(8,128)(2,1)S(1)}, u32[]{:S(2)}, u32[]{:S(2)}) %all-to-all-start.3) | async-done | bytes 2097184 | tf_op jit(solution)/shard_map/all_to_all | solution.py:81
  226.5 1.1 reduce_sum.25
  (29 shorter events, 0.4 us)
Async XLA Ops:
  9.7 8.8 %copy-start.4 = (s32[8,7]{1,0:T(8,128)S(1)}, s32[8,7]{1,0:T(8,128)}, u32[]{:S(2)}) copy-start(s32[8,7]{1,0:T(8,128)} %param.16) | copy-start | bytes 676
  9.7 8.9 %copy-start.5 = (s32[8,7]{1,0:T(8,128)S(1)}, s32[8,7]{1,0:T(8,128)}, u32[]{:S(2)}) copy-start(s32[8,7]{1,0:T(8,128)} %param.17) | copy-start | bytes 676
  9.7 39.8 %all-to-all-start = ((bf16[16,64,1024]{2,1,0:T(8,128)(2,1)}), bf16[16,64,1024]{2,1,0:T(8,128)(2,1)}, u32[]{:S(2)}, u32[]{:S(2)}) async-start(bf16[16,64,1024]{2,1,0:T(8,128)(2,1)} %broadcast_in_dim.83), calls=%async_computation | async-start | bytes 4194304 | tf_op jit(solution)/shard_map/all_to_all | solution.py:88
  18.5 86.7 %reduce-scatter.2.cloned.1.call-start = ((), (), s32[]{:S(2)}) async-start(), calls=%async_computation.5 | async-start | bytes 8257536 | tf_op jit(solution)/shard_map/reduce_scatter | solution.py:32
  59.1 0.9 copy-start.3
  61.7 4.0 %copy-start.6 = (s32[7,8]{1,0:T(8,128)S(1)}, s32[7,8]{1,0:T(8,128)}, u32[]{:S(2)}) copy-start(s32[7,8]{1,0:T(8,128)} %param.18) | copy-start | bytes 676
  61.7 32.6 %all-to-all-start.1 = ((bf16[16,64,1024]{2,1,0:T(8,128)(2,1)}), bf16[16,64,1024]{2,1,0:T(8,128)(2,1)S(1)}, u32[]{:S(2)}, u32[]{:S(2)}) async-start(bf16[16,64,1024]{2,1,0:T(8,128)(2,1)} %broadcast_in_dim.84), calls=%async_computation.2 | async-start | bytes 4194304 | tf_op jit(solution)/shard_map/all_to_all | solution.py:88
  65.6 73.8 %all-gather.3.cloned.1.call-start = ((), (), s32[]{:S(2)}) async-start(), calls=%async_computation.6 | async-start | bytes 2064384 | tf_op jit(solution)/shard_map/all_gather | solution.py:38
  94.2 8.7 %copy-start.2 = (bf16[16,64,1024]{2,1,0:T(8,128)(2,1)}, bf16[16,64,1024]{2,1,0:T(8,128)(2,1)S(1)}, u32[]{:S(2)}) copy-start(bf16[16,64,1024]{2,1,0:T(8,128)(2,1)S(1)} %all-to-all-done.1) | copy-start | bytes 6291460
  107.1 70.3 %all-gather.5.cloned.1.call-start = ((), (), s32[]{:S(2)}) async-start(), calls=%async_computation.7 | async-start | bytes 4128768 | tf_op jit(solution)/shard_map/all_gather | solution.py:38
  110.6 5.9 %collective-permute-start = (bf16[4,128,896]{1,2,0:T(8,128)(2,1)}, bf16[4,128,896]{1,2,0:T(8,128)(2,1)}, u32[]{:S(2)}, u32[]{:S(2)}) collective-permute-start(bf16[4,128,896]{1,2,0:T(8,128)(2,1)} %bitcast_convert_fusion), channel_id=1, source_target_pairs={{0,16},{16,0},{32,48},{48,32},{64,80},{80,64},{96,112},{112,96},{1... | collective-permute-start | bytes 2752520 | tf_op jit(solution)/shard_map/ppermute | solution.py:60
  119.1 20.3 %copy-start.1 = (f32[128,1792]{0,1:T(8,128)S(1)}, f32[128,1792]{0,1:T(8,128)}, u32[]{:S(2)}) copy-start(f32[128,1792]{0,1:T(8,128)} %reduce-scatter.2.cloned.1.call-done) | copy-start | bytes 2752516
  119.2 11.5 %collective-permute-start.1 = (bf16[128,896]{0,1:T(8,128)(2,1)S(1)}, bf16[128,896]{0,1:T(8,128)(2,1)S(1)}, u32[]{:S(2)}, u32[]{:S(2)}) collective-permute-start(bf16[128,896]{0,1:T(8,128)(2,1)S(1)} %get-tuple-element.66), channel_id=1, source_target_pairs={{0,32},{16,48},{32,64},{48,80},{64,96},{80,112},{96,0},{112,16},{1... | collective-permute-start | bytes 688136 | tf_op jit(solution)/shard_map/ppermute | solution.py:66
  120.3 10.4 %collective-permute-start.3 = (bf16[128,896]{0,1:T(8,128)(2,1)S(1)}, bf16[128,896]{0,1:T(8,128)(2,1)S(1)}, u32[]{:S(2)}, u32[]{:S(2)}) collective-permute-start(bf16[128,896]{0,1:T(8,128)(2,1)S(1)} %get-tuple-element.67), channel_id=1, source_target_pairs={{0,96},{16,112},{32,0},{48,16},{64,32},{80,48},{96,64},{112,80},{1... | collective-permute-start | bytes 688136 | tf_op jit(solution)/shard_map/ppermute | solution.py:66
  121.9 16.3 %collective-permute-start.2 = (bf16[128,896]{0,1:T(8,128)(2,1)S(1)}, bf16[128,896]{0,1:T(8,128)(2,1)S(1)}, u32[]{:S(2)}, u32[]{:S(2)}) collective-permute-start(bf16[128,896]{0,1:T(8,128)(2,1)S(1)} %get-tuple-element.68), channel_id=1, source_target_pairs={{0,64},{16,80},{32,96},{48,112},{64,0},{80,16},{96,32},{112,48},{1... | collective-permute-start | bytes 688136 | tf_op jit(solution)/shard_map/ppermute | solution.py:66
  146.3 40.4 %all-to-all-start.2 = ((bf16[16,64,1024]{2,1,0:T(8,128)(2,1)}), bf16[16,64,1024]{2,1,0:T(8,128)(2,1)S(1)}, u32[]{:S(2)}, u32[]{:S(2)}) async-start(bf16[16,64,1024]{2,1,0:T(8,128)(2,1)} %bitcast.68), calls=%async_computation.3 | async-start | bytes 4194304 | tf_op jit(solution)/shard_map/all_to_all | solution.py:81
  186.7 1.3 copy-start
  188.0 38.5 %all-to-all-start.3 = ((bf16[16,64,1024]{2,1,0:T(8,128)(2,1)}), bf16[16,64,1024]{2,1,0:T(8,128)(2,1)S(1)}, u32[]{:S(2)}, u32[]{:S(2)}) async-start(bf16[16,64,1024]{2,1,0:T(8,128)(2,1)} %bitcast.67), calls=%async_computation.4 | async-start | bytes 4194304 | tf_op jit(solution)/shard_map/all_to_all | solution.py:81
Sparse Core Ops, SparseCore 0:
  59.3 45.7 reduce-scatter.1
  107.2 32.0 all-gather.2
  141.6 35.6 all-gather.4
where the time goes:
time: 235 us; the launch traced here: 234 us
  waiting for transfers between devices  97.3 us (41%)
  matrix products  42 us (18%)
  starting transfers between devices  31.8 us (14%)
  local copies, waits for them, and re-layouts  30.7 us (13%)
  other arithmetic  18.4 us (8%)
  between operations  13.9 us (6%)
    all_to_all x2, waiting for transfers between devices, group_gather(): pieces = lax.all_to_all(copies, ('col', 'depth'), 0, 0)  48.8 us
    all_gather x2, waiting for transfers between devices, row_gather(): return lax.all_gather(block, 'row', axis=0, tiled=True)  23.3 us
    unnamed x24, local copies, waits for them, and re-layouts  19.1 us
    ppermute x3, waiting for transfers between devices, row_sums_paired(): lax.ppermute(piece, 'row', [(i, (i + 2 * hop) % parts) for i in range(par...  15 us
    all_to_all x2, starting transfers between devices, group_sums(): lax.all_to_all(full.reshape((parts, rows) + full.shape[1:]), ('col', 'dep...  13.7 us
    all_to_all x2, starting transfers between devices, group_gather(): pieces = lax.all_to_all(copies, ('col', 'depth'), 0, 0)  12.7 us
    dot_general x1, matrix products, local(): hidden = jnp.dot(x_all, w_both, preferred_element_type=jnp.float32)  9.65 us
    dot_general x1, matrix products, input_term(): lax.dot_general(grads_all, w_both, outer, preferred_element_type=jnp.floa...  8.52 us
  transfers between devices with their start and end apart: 11, of which 8 were waited for; matrix products, arithmetic and copies ran while one was open for 31% of the time, Pallas kernels for 0%

commit v1 on v0

--- a/solution.py
+++ b/solution.py
@@ -4,6 +4,28 @@
 from jax.sharding import PartitionSpec as P
 
 BLK = 128
+
+
+def in_order(blocks, dim):
+    lengths = list(blocks.shape[1:])
+    lengths[dim] *= blocks.shape[0]
+    return jnp.moveaxis(blocks, 0, dim).reshape(lengths)
+
+
+def ring_gather(x, axis, dim):
+    size = lax.axis_size(axis)
+    pairs = [(i, (i + 1) % size) for i in range(size)]
+    back = [(b, a) for a, b in pairs]
+    lower, upper = ([], [])
+    for step in range(size - 1):
+        if step % 2 == 0:
+            lower.append(lax.ppermute(lower[-1] if lower else x, axis, pairs))
+        else:
+            upper.append(lax.ppermute(upper[-1] if upper else x, axis, back))
+    blocks = jnp.stack([*lower[::-1], x, *upper])
+    shift = lax.axis_index(axis) - len(lower)
+    blocks = blocks[(jnp.arange(size) - shift) % size]
+    return in_order(blocks, dim)
 
 
 def expand(mask):
@@ -35,7 +57,7 @@
 
 
 def row_gather(block):
-    return lax.all_gather(block, "row", axis=0, tiled=True)
+    return ring_gather(block, "row", 0)
 
 
 def row_sums_direct(full):

time: 235 us -> 271 us (1.15)
  the two profiles are of different devices: /device:TPU:1 before, /device:TPU:3 now
where the time goes in v1:
time: 271 us; the launch traced here: 270 us
  waiting for transfers between devices  85.4 us (32%)
  local copies, waits for them, and re-layouts  62.9 us (23%)
  starting transfers between devices  48.7 us (18%)
  matrix products  41.5 us (15%)
  other arithmetic  17.1 us (6%)
  between operations  14.4 us (5%)
    all_to_all x2, waiting for transfers between devices, group_gather(): pieces = lax.all_to_all(copies, ('col', 'depth'), 0, 0)  48.8 us
    unnamed x60, local copies, waits for them, and re-layouts  34 us
    ppermute x8, waiting for transfers between devices, ring_gather(): lower.append(lax.ppermute(lower[-1] if lower else x, axis, pairs))  22.1 us
    ppermute x8, starting transfers between devices, ring_gather(): lower.append(lax.ppermute(lower[-1] if lower else x, axis, pairs))  16.8 us
    gather x4, local copies, waits for them, and re-layouts, ring_gather(): blocks = blocks[(jnp.arange(size) - shift) % size]  15.8 us
    all_to_all x2, waiting for transfers between devices, group_sums(): lax.all_to_all(full.reshape((parts, rows) + full.shape[1:]), ('col', 'dep...  13.5 us
    all_to_all x2, starting transfers between devices, group_gather(): pieces = lax.all_to_all(copies, ('col', 'depth'), 0, 0)  11.9 us
    all_to_all x2, starting transfers between devices, group_sums(): lax.all_to_all(full.reshape((parts, rows) + full.shape[1:]), ('col', 'dep...  11.7 us
  transfers between devices with their start and end apart: 23, of which 10 were waited for; matrix products, arithmetic and copies ran while one was open for 36% of the time, Pallas kernels for 0%

profile of v1, /device:TPU:3, one launch (start us, length us, event | category | flops | bytes accessed | tf_op | source)
XLA Modules:
  0.0 270.1 jit_solution(11337239799262810410)
XLA Ops:
  7.2 2.5 broadcast_in_dim.85
  9.7 8.0 %all-to-all-start = ((bf16[16,64,1024]{2,1,0:T(8,128)(2,1)}), bf16[16,64,1024]{2,1,0:T(8,128)(2,1)}, u32[]{:S(2)}, u32[]{:S(2)}) async-start(bf16[16,64,1024]{2,1,0:T(8,128)(2,1)} %broadcast_in_dim.85), calls=%async_computation | async-start | bytes 4194304 | tf_op jit(solution)/shard_map/all_to_all | solution.py:110
  18.1 2.9 %copy.20 = bf16[1024,896]{0,1:T(8,128)(2,1)S(1)} copy(bf16[1024,896]{1,0:T(8,128)(2,1)} %param.13) | data formatting | bytes 3670016 | tf_op args[1]
  21.0 3.8 %copy.22 = bf16[1024,896]{0,1:T(8,128)(2,1)} copy(bf16[1024,896]{1,0:T(8,128)(2,1)} %param.14) | data formatting | bytes 3670016 | tf_op args[2]
  24.8 3.6 %bitcast_select_fusion.1 = (bf16[1024,896]{0,1:T(8,128)(2,1)}, bf16[1024,896]{0,1:T(8,128)(2,1)}) fusion(bf16[1024,896]{0,1:T(8,128)(2,1)} %copy.22, pred[1024,7]{0,1:T(8,128)(4,1)S(1)} %bitcast.117, bf16[1024,896]{0,1:T(8,128)(2,1)S(1)} %copy.20, pred[1024,7]{0,1:T(8,128)(4,1)S(1)} %bitcast.119), kind=kLoop, calls=%fused_computation.3 | loop fusion | flops 1835008 | bytes 7354368 | tf_op jit(solution)/shard_map/jit(_where)/select_n | solution.py:120
  28.4 20.2 %all-to-all-done = bf16[16,64,1024]{2,1,0:T(8,128)(2,1)} async-done(((bf16[16,64,1024]{2,1,0:T(8,128)(2,1)}), bf16[16,64,1024]{2,1,0:T(8,128)(2,1)}, u32[]{:S(2)}, u32[]{:S(2)}) %all-to-all-start) | async-done | bytes 2097184 | tf_op jit(solution)/shard_map/all_to_all | solution.py:110
  48.7 9.6 %convolution_bitcast_fusion.1 = f32[1024,1792]{0,1:T(8,128)} fusion(bf16[1024,1024]{1,0:T(8,128)(2,1)} %bitcast.2, bf16[1024,896]{0,1:T(8,128)(2,1)} %get-tuple-element.69, bf16[1024,896]{0,1:T(8,128)(2,1)} %get-tuple-element.70), kind=kOutput, calls=%fused_computation.7 | convolution fusion | flops 3765436416 | bytes 13107200 | tf_op jit(solution)/shard_map/dot_general | solution.py:129
  60.8 3.9 %all-to-all-start.1 = ((bf16[16,64,1024]{2,1,0:T(8,128)(2,1)}), bf16[16,64,1024]{2,1,0:T(8,128)(2,1)S(1)}, u32[]{:S(2)}, u32[]{:S(2)}) async-start(bf16[16,64,1024]{2,1,0:T(8,128)(2,1)} %broadcast_in_dim.86), calls=%async_computation.2 | async-start | bytes 4194304 | tf_op jit(solution)/shard_map/all_to_all | solution.py:110
  64.8 28.6 %all-to-all-done.1 = bf16[16,64,1024]{2,1,0:T(8,128)(2,1)S(1)} async-done(((bf16[16,64,1024]{2,1,0:T(8,128)(2,1)}), bf16[16,64,1024]{2,1,0:T(8,128)(2,1)S(1)}, u32[]{:S(2)}, u32[]{:S(2)}) %all-to-all-start.1) | async-done | bytes 2097184 | tf_op jit(solution)/shard_map/all_to_all | solution.py:110
  93.4 2.8 %broadcast_in_dim.88 = pred[896,8,128]{2,1,0:T(8,128)(4,1)S(1)} broadcast(pred[896,8]{1,0:T(8,128)(4,1)S(1)} %bitcast.116), dimensions={0,1} | broadcast | bytes 924672 | tf_op jit(solution)/shard_map/broadcast_in_dim | solution.py:32
  97.2 5.9 %fusion.4 = f32[1024,896]{1,0:T(8,128)} fusion(bf16[1024,1024]{1,0:T(8,128)(2,1)S(1)} %bitcast.103, bf16[896,1024]{1,0:T(8,128)(2,1)} %param.15, pred[112,8,8,128]{3,2,1,0:T(8,128)(4,1)S(1)} %bitcast.113), kind=kOutput, calls=%fused_computation.18 | convolution fusion | flops 1879965696 | bytes 8519680 | tf_op jit(solution)/shard_map/dot_general | solution.py:133
  107.3 2.2 collective-permute-start.7
  110.8 3.0 %collective-permute-done = bf16[128,896]{0,1:T(8,128)(2,1)S(1)} collective-permute-done((bf16[128,896]{0,1:T(8,128)(2,1)S(1)}, bf16[128,896]{0,1:T(8,128)(2,1)S(1)}, u32[]{:S(2)}, u32[]{:S(2)}) %collective-permute-start) | collective-permute-done | bytes 229408 | tf_op jit(solution)/shard_map/ppermute | solution.py:22
  113.8 2.5 collective-permute-start.1
  116.3 2.9 %collective-permute-done.1 = bf16[128,896]{0,1:T(8,128)(2,1)S(1)} collective-permute-done((bf16[128,896]{0,1:T(8,128)(2,1)S(1)}, bf16[128,896]{0,1:T(8,128)(2,1)S(1)}, u32[]{:S(2)}, u32[]{:S(2)}) %collective-permute-start.1) | collective-permute-done | bytes 229408 | tf_op jit(solution)/shard_map/ppermute | solution.py:22
  119.2 2.5 collective-permute-start.2
  121.7 2.9 %constant_dynamic-slice_fusion.1 = f32[4,1,128,896]{3,2,1,0:T(8,128)} fusion(f32[4,2,128,896]{3,2,1,0:T(8,128)} %bitcast.110, s32[]{:T(128)S(6)} %select_n.120), kind=kLoop, calls=%fused_computation.61 | loop fusion | bytes 3670020 | tf_op jit(solution)/shard_map/jit(_take) | solution.py:81
  124.6 1.8 copy.29
  126.4 1.7 collective-permute-start.3
  128.2 2.7 fusion.15
  132.5 4.4 %collective-permute-start.9 = (bf16[128,896]{0,1:T(8,128)(2,1)S(1)}, bf16[128,896]{0,1:T(8,128)(2,1)}, u32[]{:S(2)}, u32[]{:S(2)}) collective-permute-start(bf16[128,896]{0,1:T(8,128)(2,1)S(1)} %get-tuple-element.68), channel_id=1, source_target_pairs={{0,64},{16,80},{32,96},{48,112},{64,0},{80,16},{96,32},{112,48},{1... | collective-permute-start | bytes 688136 | tf_op jit(solution)/shard_map/ppermute | solution.py:88
  137.6 1.6 bitcast_dynamic-update-slice_fusion.13
  142.2 1.6 bitcast_dynamic-update-slice_fusion.8
  144.5 2.4 gather_fusion
  147.0 2.6 copy.23
  152.9 5.4 %collective-permute-done.11 = bf16[128,1792]{0,1:T(8,128)(2,1)S(1)} collective-permute-done((bf16[128,1792]{0,1:T(8,128)(2,1)S(1)}, bf16[128,1792]{0,1:T(8,128)(2,1)S(1)}, u32[]{:S(2)}, u32[]{:S(2)}) %collective-permute-start.11) | collective-permute-done | bytes 458784 | tf_op jit(solution)/shard_map/ppermute | solution.py:22
  159.1 2.5 collective-permute-start.12
  161.6 5.4 %collective-permute-done.12 = bf16[128,1792]{0,1:T(8,128)(2,1)S(1)} collective-permute-done((bf16[128,1792]{0,1:T(8,128)(2,1)S(1)}, bf16[128,1792]{0,1:T(8,128)(2,1)S(1)}, u32[]{:S(2)}, u32[]{:S(2)}) %collective-permute-start.12) | collective-permute-done | bytes 458784 | tf_op jit(solution)/shard_map/ppermute | solution.py:22
  167.8 2.5 collective-permute-start.13
  170.3 5.4 %collective-permute-done.13 = bf16[128,1792]{0,1:T(8,128)(2,1)} collective-permute-done((bf16[128,1792]{0,1:T(8,128)(2,1)S(1)}, bf16[128,1792]{0,1:T(8,128)(2,1)}, u32[]{:S(2)}, u32[]{:S(2)}) %collective-permute-start.13) | collective-permute-done | bytes 458784 | tf_op jit(solution)/shard_map/ppermute | solution.py:22
  175.7 2.6 collective-permute-start.14
  178.3 5.3 %convolution_convert_fusion = bf16[1024,1024]{1,0:T(8,128)(2,1)} fusion(bf16[1024,896]{1,0:T(8,128)(2,1)S(1)} %bitcast.112, bf16[896,1024]{1,0:T(8,128)(2,1)} %param.15, pred[112,8,8,128]{3,2,1,0:T(8,128)(4,1)S(1)} %bitcast.114), kind=kOutput, calls=%fused_computation.15 | convolution fusion | flops 1881014272 | bytes 6684672 | tf_op jit(solution)/shard_map/dot_general | solution.py:138
  183.6 6.0 %all-to-all-start.2 = ((bf16[16,64,1024]{2,1,0:T(8,128)(2,1)}), bf16[16,64,1024]{2,1,0:T(8,128)(2,1)S(1)}, u32[]{:S(2)}, u32[]{:S(2)}) async-start(bf16[16,64,1024]{2,1,0:T(8,128)(2,1)} %bitcast.105), calls=%async_computation.3 | async-start | bytes 4194304 | tf_op jit(solution)/shard_map/all_to_all | solution.py:103
  189.7 1.9 bitcast_dynamic-update-slice_fusion.6
  191.6 1.8 bitcast_dynamic-update-slice_fusion.5
  195.8 1.8 bitcast_dynamic-update-slice_fusion.2
  197.6 1.8 bitcast_dynamic-update-slice_fusion.1
  200.3 4.9 %gather_fusion.1 = bf16[8,128,1792]{1,2,0:T(8,128)(2,1)} fusion(bf16[8,128,1792]{1,2,0:T(8,128)(2,1)} %bitcast_dynamic-update-slice_fusion, s32[1024]{0:T(1024)S(1)} %pad_clamp_fusion), kind=kCustom, calls=%fused_computation.1 | custom fusion | bytes 7340064 | tf_op jit(solution)/shard_map/gather | solution.py:27
  205.1 5.9 %copy.26 = bf16[8,128,1792]{2,1,0:T(8,128)(2,1)} copy(bf16[8,128,1792]{1,2,0:T(8,128)(2,1)} %gather_fusion.1) | data formatting | bytes 7340032 | tf_op jit(solution)/shard_map/gather | solution.py:27
  211.0 8.4 %fusion.3 = bf16[1024,1024]{1,0:T(8,128)(2,1)} fusion(bf16[1024,1792]{1,0:T(8,128)(2,1)} %bitcast.101, bf16[1024,896]{0,1:T(8,128)(2,1)} %get-tuple-element.69, bf16[1024,896]{0,1:T(8,128)(2,1)} %get-tuple-element.70), kind=kOutput, calls=%fused_computation.14 | convolution fusion | flops 3766484992 | bytes 9437184 | tf_op jit(solution)/shard_map/dot_general | solution.py:154
  220.5 5.7 %all-to-all-start.3 = ((bf16[16,64,1024]{2,1,0:T(8,128)(2,1)}), bf16[16,64,1024]{2,1,0:T(8,128)(2,1)}, u32[]{:S(2)}, u32[]{:S(2)}) async-start(bf16[16,64,1024]{2,1,0:T(8,128)(2,1)} %bitcast.106), calls=%async_computation.4 | async-start | bytes 4194304 | tf_op jit(solution)/shard_map/all_to_all | solution.py:103
  226.2 5.6 %select_convert_fusion = bf16[896,1024]{1,0:T(8,128)(2,1)} fusion(pred[112,8,8,128]{3,2,1,0:T(8,128)(4,1)S(1)} %bitcast.115, bf16[1024,896]{1,0:T(8,128)(2,1)} %bitcast.111, bf16[1024,1024]{1,0:T(8,128)(2,1)} %bitcast.104), kind=kOutput, calls=%fused_computation.11 | convolution fusion | flops 1880883200 | bytes 6684672 | tf_op jit(solution)/shard_map/dot_general | solution.py:141
  232.8 6.7 %convolution_bitcast_fusion = bf16[1024,1792]{0,1:T(8,128)(2,1)S(1)} fusion(bf16[1024,1792]{1,0:T(8,128)(2,1)} %bitcast.102, bf16[1024,1024]{1,0:T(8,128)(2,1)} %bitcast.2), kind=kOutput, calls=%fused_computation.6 | convolution fusion | flops 3758096384 | bytes 9437184 | tf_op jit(solution)/shard_map/dot_general | solution.py:146
  239.6 2.3 fusion.1
  241.9 3.8 %copy.28 = bf16[1024,896]{1,0:T(8,128)(2,1)} copy(bf16[1024,896]{0,1:T(8,128)(2,1)} %get-tuple-element.62) | data formatting | bytes 3670016
  245.7 2.4 copy.27
  248.1 12.4 %all-to-all-done.3 = bf16[16,64,1024]{2,1,0:T(8,128)(2,1)} async-done(((bf16[16,64,1024]{2,1,0:T(8,128)(2,1)}), bf16[16,64,1024]{2,1,0:T(8,128)(2,1)}, u32[]{:S(2)}, u32[]{:S(2)}) %all-to-all-start.3) | async-done | bytes 2097184 | tf_op jit(solution)/shard_map/all_to_all | solution.py:103
  260.5 2.7 reduce_sum.25
  (97 shorter events, 25.7 us)
Async XLA Ops:
  9.7 8.0 %copy-start.16 = (s32[8,7]{1,0:T(8,128)S(1)}, s32[8,7]{1,0:T(8,128)}, u32[]{:S(2)}) copy-start(s32[8,7]{1,0:T(8,128)} %param.16) | copy-start | bytes 676
  9.7 8.1 %copy-start.17 = (s32[8,7]{1,0:T(8,128)S(1)}, s32[8,7]{1,0:T(8,128)}, u32[]{:S(2)}) copy-start(s32[8,7]{1,0:T(8,128)} %param.17) | copy-start | bytes 676
  9.7 39.0 %all-to-all-start = ((bf16[16,64,1024]{2,1,0:T(8,128)(2,1)}), bf16[16,64,1024]{2,1,0:T(8,128)(2,1)}, u32[]{:S(2)}, u32[]{:S(2)}) async-start(bf16[16,64,1024]{2,1,0:T(8,128)(2,1)} %broadcast_in_dim.85), calls=%async_computation | async-start | bytes 4194304 | tf_op jit(solution)/shard_map/all_to_all | solution.py:110
  17.7 86.3 %reduce-scatter.2.cloned.1.call-start = ((), (), s32[]{:S(2)}) async-start(), calls=%async_computation.5 | async-start | bytes 8257536 | tf_op jit(solution)/shard_map/reduce_scatter | solution.py:54
  58.3 0.9 copy-start.15
  60.8 4.0 %copy-start.18 = (s32[7,8]{1,0:T(8,128)S(1)}, s32[7,8]{1,0:T(8,128)}, u32[]{:S(2)}) copy-start(s32[7,8]{1,0:T(8,128)} %param.18) | copy-start | bytes 676
  60.8 32.6 %all-to-all-start.1 = ((bf16[16,64,1024]{2,1,0:T(8,128)(2,1)}), bf16[16,64,1024]{2,1,0:T(8,128)(2,1)S(1)}, u32[]{:S(2)}, u32[]{:S(2)}) async-start(bf16[16,64,1024]{2,1,0:T(8,128)(2,1)} %broadcast_in_dim.86), calls=%async_computation.2 | async-start | bytes 4194304 | tf_op jit(solution)/shard_map/all_to_all | solution.py:110
  93.4 9.6 %copy-start.1 = (bf16[16,64,1024]{2,1,0:T(8,128)(2,1)}, bf16[16,64,1024]{2,1,0:T(8,128)(2,1)S(1)}, u32[]{:S(2)}) copy-start(bf16[16,64,1024]{2,1,0:T(8,128)(2,1)S(1)} %all-to-all-done.1) | copy-start | bytes 6291460
  96.2 0.9 copy-start.3
  105.6 4.0 %copy-start = (f32[128,1792]{0,1:T(8,128)S(1)}, f32[128,1792]{0,1:T(8,128)}, u32[]{:S(2)}) copy-start(f32[128,1792]{0,1:T(8,128)} %reduce-scatter.2.cloned.1.call-done) | copy-start | bytes 2752516
  107.3 20.8 %collective-permute-start.7 = (bf16[4,128,896]{1,2,0:T(8,128)(2,1)}, bf16[4,128,896]{1,2,0:T(8,128)(2,1)}, u32[]{:S(2)}, u32[]{:S(2)}) collective-permute-start(bf16[4,128,896]{1,2,0:T(8,128)(2,1)} %bitcast_convert_fusion), channel_id=1, source_target_pairs={{0,16},{16,0},{32,48},{48,32},{64,80},{80,64},{96,112},{112,96},{1... | collective-permute-start | bytes 2752520 | tf_op jit(solution)/shard_map/ppermute | solution.py:82
  109.7 4.1 %collective-permute-start = (bf16[128,896]{0,1:T(8,128)(2,1)S(1)}, bf16[128,896]{0,1:T(8,128)(2,1)S(1)}, u32[]{:S(2)}, u32[]{:S(2)}) collective-permute-start(bf16[128,896]{0,1:T(8,128)(2,1)S(1)} %multiply_convert_fusion.2), channel_id=1, source_target_pairs={{0,16},{16,32},{32,48},{48,64},{64,80},{80,96},{96,112},{112,0},{1... | collective-permute-start | bytes 688136 | tf_op jit(solution)/shard_map/ppermute | solution.py:22
  110.8 5.5 %collective-permute-start.4 = (bf16[128,896]{0,1:T(8,128)(2,1)S(1)}, bf16[128,896]{0,1:T(8,128)(2,1)S(1)}, u32[]{:S(2)}, u32[]{:S(2)}) collective-permute-start(bf16[128,896]{0,1:T(8,128)(2,1)S(1)} %multiply_convert_fusion.2), channel_id=1, source_target_pairs={{16,0},{32,16},{48,32},{64,48},{80,64},{96,80},{112,96},{0,112},{1... | collective-permute-start | bytes 688136 | tf_op jit(solution)/shard_map/ppermute | solution.py:24
  113.8 7.9 %copy-start.11 = (bf16[128,896]{0,1:T(8,128)(2,1)}, bf16[128,896]{0,1:T(8,128)(2,1)S(1)}, u32[]{:S(2)}) copy-start(bf16[128,896]{0,1:T(8,128)(2,1)S(1)} %collective-permute-done) | copy-start | bytes 688132
  113.8 5.4 %collective-permute-start.1 = (bf16[128,896]{0,1:T(8,128)(2,1)S(1)}, bf16[128,896]{0,1:T(8,128)(2,1)S(1)}, u32[]{:S(2)}, u32[]{:S(2)}) collective-permute-start(bf16[128,896]{0,1:T(8,128)(2,1)S(1)} %collective-permute-done), channel_id=1, source_target_pairs={{0,16},{16,32},{32,48},{48,64},{64,80},{80,96},{96,112},{112,0},{1... | collective-permute-start | bytes 688136 | tf_op jit(solution)/shard_map/ppermute | solution.py:22
  116.3 10.1 %copy-start.9 = (bf16[128,896]{0,1:T(8,128)(2,1)}, bf16[128,896]{0,1:T(8,128)(2,1)S(1)}, u32[]{:S(2)}) copy-start(bf16[128,896]{0,1:T(8,128)(2,1)S(1)} %collective-permute-done.4) | copy-start | bytes 688132
  116.3 10.1 %collective-permute-start.5 = (bf16[128,896]{0,1:T(8,128)(2,1)S(1)}, bf16[128,896]{0,1:T(8,128)(2,1)}, u32[]{:S(2)}, u32[]{:S(2)}) collective-permute-start(bf16[128,896]{0,1:T(8,128)(2,1)S(1)} %collective-permute-done.4), channel_id=1, source_target_pairs={{16,0},{32,16},{48,32},{64,48},{80,64},{96,80},{112,96},{0,112},{1... | collective-permute-start | bytes 688136 | tf_op jit(solution)/shard_map/ppermute | solution.py:24
  119.2 7.2 %copy-start.13 = (bf16[128,896]{0,1:T(8,128)(2,1)}, bf16[128,896]{0,1:T(8,128)(2,1)S(1)}, u32[]{:S(2)}) copy-start(bf16[128,896]{0,1:T(8,128)(2,1)S(1)} %collective-permute-done.1) | copy-start | bytes 688132
  119.2 7.2 %collective-permute-start.2 = (bf16[128,896]{0,1:T(8,128)(2,1)S(1)}, bf16[128,896]{0,1:T(8,128)(2,1)}, u32[]{:S(2)}, u32[]{:S(2)}) collective-permute-start(bf16[128,896]{0,1:T(8,128)(2,1)S(1)} %collective-permute-done.1), channel_id=1, source_target_pairs={{0,16},{16,32},{32,48},{48,64},{64,80},{80,96},{96,112},{112,0},{1... | collective-permute-start | bytes 688136 | tf_op jit(solution)/shard_map/ppermute | solution.py:22
  126.4 17.4 %collective-permute-start.6 = (bf16[128,896]{0,1:T(8,128)(2,1)}, bf16[128,896]{0,1:T(8,128)(2,1)S(1)}, u32[]{:S(2)}, u32[]{:S(2)}) collective-permute-start(bf16[128,896]{0,1:T(8,128)(2,1)} %collective-permute-done.5), channel_id=1, source_target_pairs={{16,0},{32,16},{48,32},{64,48},{80,64},{96,80},{112,96},{0,112},{1... | collective-permute-start | bytes 688136 | tf_op jit(solution)/shard_map/ppermute | solution.py:24
  126.4 10.5 %collective-permute-start.3 = (bf16[128,896]{0,1:T(8,128)(2,1)}, bf16[128,896]{0,1:T(8,128)(2,1)S(1)}, u32[]{:S(2)}, u32[]{:S(2)}) collective-permute-start(bf16[128,896]{0,1:T(8,128)(2,1)} %collective-permute-done.2), channel_id=1, source_target_pairs={{0,16},{16,32},{32,48},{48,64},{64,80},{80,96},{96,112},{112,0},{1... | collective-permute-start | bytes 688136 | tf_op jit(solution)/shard_map/ppermute | solution.py:22
  130.9 8.4 %copy-start.14 = (bf16[128,896]{0,1:T(8,128)(2,1)S(1)}, bf16[128,896]{0,1:T(8,128)(2,1)}, u32[]{:S(2)}) copy-start(bf16[128,896]{0,1:T(8,128)(2,1)} %copy-done.13) | copy-start | bytes 688132
  130.9 9.1 %copy-start.12 = (bf16[128,896]{0,1:T(8,128)(2,1)S(1)}, bf16[128,896]{0,1:T(8,128)(2,1)}, u32[]{:S(2)}) copy-start(bf16[128,896]{0,1:T(8,128)(2,1)} %copy-done.11) | copy-start | bytes 688132
  130.9 10.6 %copy-start.10 = (bf16[128,896]{0,1:T(8,128)(2,1)S(1)}, bf16[128,896]{0,1:T(8,128)(2,1)}, u32[]{:S(2)}) copy-start(bf16[128,896]{0,1:T(8,128)(2,1)} %copy-done.9) | copy-start | bytes 688132
  130.9 18.7 %collective-permute-start.8 = (bf16[128,896]{0,1:T(8,128)(2,1)S(1)}, bf16[128,896]{0,1:T(8,128)(2,1)}, u32[]{:S(2)}, u32[]{:S(2)}) collective-permute-start(bf16[128,896]{0,1:T(8,128)(2,1)S(1)} %get-tuple-element.66), channel_id=1, source_target_pairs={{0,32},{16,48},{32,64},{48,80},{64,96},{80,112},{96,0},{112,16},{1... | collective-permute-start | bytes 688136 | tf_op jit(solution)/shard_map/ppermute | solution.py:88
  132.0 17.6 %collective-permute-start.10 = (bf16[128,896]{0,1:T(8,128)(2,1)S(1)}, bf16[128,896]{0,1:T(8,128)(2,1)}, u32[]{:S(2)}, u32[]{:S(2)}) collective-permute-start(bf16[128,896]{0,1:T(8,128)(2,1)S(1)} %get-tuple-element.67), channel_id=1, source_target_pairs={{0,96},{16,112},{32,0},{48,16},{64,32},{80,48},{96,64},{112,80},{1... | collective-permute-start | bytes 688136 | tf_op jit(solution)/shard_map/ppermute | solution.py:88
  132.5 17.1 %collective-permute-start.9 = (bf16[128,896]{0,1:T(8,128)(2,1)S(1)}, bf16[128,896]{0,1:T(8,128)(2,1)}, u32[]{:S(2)}, u32[]{:S(2)}) collective-permute-start(bf16[128,896]{0,1:T(8,128)(2,1)S(1)} %get-tuple-element.68), channel_id=1, source_target_pairs={{0,64},{16,80},{32,96},{48,112},{64,0},{80,16},{96,32},{112,48},{1... | collective-permute-start | bytes 688136 | tf_op jit(solution)/shard_map/ppermute | solution.py:88
  149.6 28.7 %copy-start.2 = (bf16[8,128,896]{2,1,0:T(8,128)(2,1)S(1)}, bf16[8,128,896]{2,1,0:T(8,128)(2,1)}, u32[]{:S(2)}) copy-start(bf16[8,128,896]{2,1,0:T(8,128)(2,1)} %copy.23) | copy-start | bytes 5505028
  149.6 28.7 %copy-start.4 = (pred[896,8,128]{2,1,0:T(8,128)(4,1)S(1)}, pred[896,8,128]{2,1,0:T(8,128)(4,1)}, u32[]{:S(2)}) copy-start(pred[896,8,128]{2,1,0:T(8,128)(4,1)} %copy-done.3) | copy-start | bytes 2752516
  151.4 6.9 %collective-permute-start.11 = (bf16[128,1792]{0,1:T(8,128)(2,1)S(1)}, bf16[128,1792]{0,1:T(8,128)(2,1)S(1)}, u32[]{:S(2)}, u32[]{:S(2)}) collective-permute-start(bf16[128,1792]{0,1:T(8,128)(2,1)S(1)} %pad_maximum_fusion.5), channel_id=1, source_target_pairs={{0,16},{16,32},{32,48},{48,64},{64,80},{80,96},{96,112},{112,0},{1... | collective-permute-start | bytes 1376264 | tf_op jit(solution)/shard_map/ppermute | solution.py:22
  158.3 0.8 copy-start.5
  159.1 7.9 %collective-permute-start.12 = (bf16[128,1792]{0,1:T(8,128)(2,1)S(1)}, bf16[128,1792]{0,1:T(8,128)(2,1)S(1)}, u32[]{:S(2)}, u32[]{:S(2)}) collective-permute-start(bf16[128,1792]{0,1:T(8,128)(2,1)S(1)} %collective-permute-done.11), channel_id=1, source_target_pairs={{0,16},{16,32},{32,48},{48,64},{64,80},{80,96},{96,112},{112,0},{1... | collective-permute-start | bytes 1376264 | tf_op jit(solution)/shard_map/ppermute | solution.py:22
  161.6 8.7 %collective-permute-start.15 = (bf16[128,1792]{0,1:T(8,128)(2,1)S(1)}, bf16[128,1792]{0,1:T(8,128)(2,1)}, u32[]{:S(2)}, u32[]{:S(2)}) collective-permute-start(bf16[128,1792]{0,1:T(8,128)(2,1)S(1)} %pad_maximum_fusion.5), channel_id=1, source_target_pairs={{16,0},{32,16},{48,32},{64,48},{80,64},{96,80},{112,96},{0,112},{1... | collective-permute-start | bytes 1376264 | tf_op jit(solution)/shard_map/ppermute | solution.py:24
  167.0 0.8 copy-start.7
  167.8 7.9 %collective-permute-start.13 = (bf16[128,1792]{0,1:T(8,128)(2,1)S(1)}, bf16[128,1792]{0,1:T(8,128)(2,1)}, u32[]{:S(2)}, u32[]{:S(2)}) collective-permute-start(bf16[128,1792]{0,1:T(8,128)(2,1)S(1)} %collective-permute-done.12), channel_id=1, source_target_pairs={{0,16},{16,32},{32,48},{48,64},{64,80},{80,96},{96,112},{112,0},{1... | collective-permute-start | bytes 1376264 | tf_op jit(solution)/shard_map/ppermute | solution.py:22
  170.3 19.3 %collective-permute-start.16 = (bf16[128,1792]{0,1:T(8,128)(2,1)}, bf16[128,1792]{0,1:T(8,128)(2,1)}, u32[]{:S(2)}, u32[]{:S(2)}) collective-permute-start(bf16[128,1792]{0,1:T(8,128)(2,1)} %collective-permute-done.15), channel_id=1, source_target_pairs={{16,0},{32,16},{48,32},{64,48},{80,64},{96,80},{112,96},{0,112},{1... | collective-permute-start | bytes 1376264 | tf_op jit(solution)/shard_map/ppermute | solution.py:24
  175.7 13.9 %collective-permute-start.14 = (bf16[128,1792]{0,1:T(8,128)(2,1)}, bf16[128,1792]{0,1:T(8,128)(2,1)}, u32[]{:S(2)}, u32[]{:S(2)}) collective-permute-start(bf16[128,1792]{0,1:T(8,128)(2,1)} %collective-permute-done.13), channel_id=1, source_target_pairs={{0,16},{16,32},{32,48},{48,64},{64,80},{80,96},{96,112},{112,0},{1... | collective-permute-start | bytes 1376264 | tf_op jit(solution)/shard_map/ppermute | solution.py:22
  183.6 36.9 %all-to-all-start.2 = ((bf16[16,64,1024]{2,1,0:T(8,128)(2,1)}), bf16[16,64,1024]{2,1,0:T(8,128)(2,1)S(1)}, u32[]{:S(2)}, u32[]{:S(2)}) async-start(bf16[16,64,1024]{2,1,0:T(8,128)(2,1)} %bitcast.105), calls=%async_computation.3 | async-start | bytes 4194304 | tf_op jit(solution)/shard_map/all_to_all | solution.py:103
  189.6 3.8 %copy-start.8 = (bf16[128,1792]{0,1:T(8,128)(2,1)S(1)}, bf16[128,1792]{0,1:T(8,128)(2,1)}, u32[]{:S(2)}) copy-start(bf16[128,1792]{0,1:T(8,128)(2,1)} %copy-done.7) | copy-start | bytes 1376260
  189.6 4.6 %copy-start.6 = (bf16[128,1792]{0,1:T(8,128)(2,1)S(1)}, bf16[128,1792]{0,1:T(8,128)(2,1)}, u32[]{:S(2)}) copy-start(bf16[128,1792]{0,1:T(8,128)(2,1)} %copy-done.5) | copy-start | bytes 1376260
  189.6 9.8 %collective-permute-start.17 = (bf16[128,1792]{0,1:T(8,128)(2,1)}, bf16[128,1792]{0,1:T(8,128)(2,1)S(1)}, u32[]{:S(2)}, u32[]{:S(2)}) collective-permute-start(bf16[128,1792]{0,1:T(8,128)(2,1)} %collective-permute-done.16), channel_id=1, source_target_pairs={{16,0},{32,16},{48,32},{64,48},{80,64},{96,80},{112,96},{0,112},{1... | collective-permute-start | bytes 1376264 | tf_op jit(solution)/shard_map/ppermute | solution.py:24
  220.5 40.1 %all-to-all-start.3 = ((bf16[16,64,1024]{2,1,0:T(8,128)(2,1)}), bf16[16,64,1024]{2,1,0:T(8,128)(2,1)}, u32[]{:S(2)}, u32[]{:S(2)}) async-start(bf16[16,64,1024]{2,1,0:T(8,128)(2,1)} %bitcast.106), calls=%async_computation.4 | async-start | bytes 4194304 | tf_op jit(solution)/shard_map/all_to_all | solution.py:103
Sparse Core Ops, SparseCore 0:
  58.4 45.4 reduce-scatter.1
